TPU v7x, 32 devices: a whole 2x2x4 slice. The times are simulated.
32 devices in a mesh: rep: 4 (over x, core), frame: 4 (over z), row: 2 (over y).
Axes of the slice: x: 2, y: 2, z: 4, core: 2. Of those that a mesh axis runs over, the one named last changes fastest.
Arguments:
- activations: bfloat16 [4, 4, 16, 32, 1280], P('rep', 'frame', 'row'), may hold values from -70 to 70, as said below
- spatial_weight: bfloat16 [9, 1280, 1280], P(None, None, ('rep', 'frame')), may hold values from -0.0546875 to 0.0546875
- temporal_weight: bfloat16 [3, 1280, 1280], P(None, None, ('rep', 'frame')), may hold values from -0.09375 to 0.09375
- first_gain: float32 [1280], replicated, may hold values from 0.25 to 1.75
- first_shift: float32 [1280], replicated, may hold values from -1.5 to 1.5
- spatial_bias: float32 [1280], replicated, may hold values from -2.5 to 2.5
- second_gain: float32 [1280], replicated, may hold values from 0.25 to 1.75
- second_shift: float32 [1280], replicated, may hold values from -1.5 to 1.5
- temporal_bias: float32 [1280], replicated, may hold values from -1.5 to 1.5
Outputs:
- block_out: float32 [4, 4, 16, 32, 1280], P('rep', 'frame', 'row')
Inputs may be any that keep to these rules, and one draw needn't show every extreme that they name: `activations`: finite values.
All inputs are finite; a program needn't handle non-finite values.
Results may differ from a plain program's by a relative error of at most 0.0009.
Values may be sent and summed in bfloat16 or wider, within the bound.
No kernel may reach another device: no remote copies, remote signals or barrier semaphores. Data moves between devices by JAX's collectives and lax.ppermute only.
A program may use at most 128 MiB of HBM per device.

v0:
```python
import jax
import jax.numpy as jnp
from jax import lax
from jax.sharding import PartitionSpec as P

GROUPS = 32
EPS = 1e-05


def padded_2(block, sides, width):
    for axis, dim in sides:
        count = lax.axis_size(axis)
        forward = [(i, i + 1) for i in range(count - 1)]
        backward = [(target, source) for source, target in forward]
        low = lax.ppermute(
            lax.slice_in_dim(block, block.shape[dim] - width, None, axis=dim), axis, forward
        )
        high = lax.ppermute(lax.slice_in_dim(block, 0, width, axis=dim), axis, backward)
        block = jnp.concatenate([low, block, high], axis=dim)
    return block


def norm_silu(field, gain, shift):
    samples = field.shape[0]
    width = field.shape[-1] // GROUPS
    grouped = field.reshape(samples, -1, GROUPS, width)
    sums = jnp.sum(grouped, axis=(1, 3))
    squares = jnp.sum(grouped * grouped, axis=(1, 3))
    sums, squares = lax.psum((sums, squares), ("frame", "row"))
    count = grouped.shape[1] * width * lax.axis_size("frame") * lax.axis_size("row")
    mean = sums / count
    variance = squares / count - mean * mean
    inverse = lax.rsqrt(variance + EPS)
    mean_full = jnp.repeat(mean, width, axis=1)[:, None, None, None, :]
    inverse_full = jnp.repeat(inverse, width, axis=1)[:, None, None, None, :]
    normed = (field - mean_full) * inverse_full * gain + shift
    return jax.nn.silu(normed).astype(jnp.bfloat16)


def conv_taps(padded, weights, rows, cols):
    leading = padded.shape[0] * padded.shape[1]
    channels = padded.shape[-1]
    summed = jnp.zeros((leading * rows * cols, weights.shape[-1]), jnp.float32)
    for row_tap in range(3):
        for col_tap in range(3):
            section = padded[:, :, row_tap : row_tap + rows, col_tap : col_tap + cols, :].reshape(
                -1, channels
            )
            summed = summed + jnp.dot(
                section, weights[3 * row_tap + col_tap], preferred_element_type=jnp.float32
            )
    return summed.reshape(padded.shape[0], padded.shape[1], rows, cols, -1)


def time_taps(window, weights, frames_dev):
    channels = window.shape[-1]
    samples, rows, cols = (window.shape[0], window.shape[2], window.shape[3])
    summed = jnp.zeros((samples * frames_dev * rows * cols, weights.shape[-1]), jnp.float32)
    for tap in range(3):
        section = window[:, tap : tap + frames_dev].reshape(-1, channels)
        summed = summed + jnp.dot(section, weights[tap], preferred_element_type=jnp.float32)
    return summed.reshape(samples, frames_dev, rows, cols, -1)


def shards(
    activations,
    spatial_weight,
    temporal_weight,
    first_gain,
    first_shift,
    spatial_bias,
    second_gain,
    second_shift,
    temporal_bias,
):
    frames_dev = activations.shape[1]
    rows_dev = activations.shape[2]
    cols = activations.shape[3]
    inputs = activations.astype(jnp.float32)
    first = norm_silu(inputs, first_gain, first_shift)
    with_rims = padded_2(first, (("row", 2),), 1)
    gathered = lax.all_gather(with_rims, "rep", axis=0, tiled=True)
    padded = jnp.pad(gathered, ((0, 0), (0, 0), (0, 0), (1, 1), (0, 0)))
    quarter = conv_taps(
        padded, lax.all_gather(spatial_weight, "frame", axis=2, tiled=True), rows_dev, cols
    )
    spatial = lax.all_to_all(
        quarter.astype(jnp.bfloat16), "rep", split_axis=0, concat_axis=4, tiled=True
    ).astype(quarter.dtype)
    spatial = spatial + spatial_bias
    second = norm_silu(spatial, second_gain, second_shift)
    window = padded_2(second, (("frame", 1),), 1)
    window_all = lax.all_gather(window, "rep", axis=0, tiled=True)
    quarter_time = time_taps(
        window_all, lax.all_gather(temporal_weight, "frame", axis=2, tiled=True), frames_dev
    )
    temporal = lax.all_to_all(
        quarter_time.astype(jnp.bfloat16), "rep", split_axis=0, concat_axis=4, tiled=True
    ).astype(quarter_time.dtype)
    return inputs + temporal + temporal_bias


def solution(mesh):
    placed = (
        P("rep", "frame", "row", None, None),
        P(None, None, ("rep", "frame")),
        P(None, None, ("rep", "frame")),
        P(),
        P(),
        P(),
        P(),
        P(),
        P(),
    )
    return jax.shard_map(
        shards,
        mesh=mesh,
        in_specs=placed,
        out_specs=P("rep", "frame", "row", None, None),
        check_vma=False,
    )
```

profile of v0, /device:TPU:0, one launch (start us, length us, event | category | flops | bytes accessed | tf_op | source)
XLA Modules:
  0.0 412.9 jit_solution(1252224786105186306)
XLA Ops:
  6.5 1.3 convert_reduce_fusion
  8.2 23.2 %all-reduce.2 = (f32[1,32]{1,0:T(1,128)S(1)}, f32[1,32]{1,0:T(1,128)S(1)}) all-reduce(f32[1,32]{1,0:T(1,128)S(1)} %bitcast.114, f32[1,32]{1,0:T(1,128)S(1)} %bitcast.112), channel_id=1, replica_groups=mesh['rep'=4,'frame'=4,'row'=2] {'frame','row'}, use_global_device_ids=true, to_apply=%region_5.6 | all-reduce | flops 64 | bytes 512 | tf_op jit(solution)/shard_map/psum | solution.py:29
  31.7 1.6 fusion.14
  33.3 1.3 collective-permute-start
  34.6 1.3 collective-permute-start.1
  35.9 0.7 collective-permute-done
  36.6 4.3 %collective-permute-done.1 = bf16[1,1,1,32,1280]{4,3,2,1,0:T(8,128)(2,1)S(1)} collective-permute-done((bf16[1,1,1,32,1280]{4,3,2,1,0:T(8,128)(2,1)S(1)}, bf16[1,1,1,32,1280]{4,3,2,1,0:T(8,128)(2,1)S(1)}, u32[]{:S(2)}, u32[]{:S(2)}) %collective-permute-start.1) | collective-permute-done | bytes 81952 | tf_op jit(solution)/shard_map/ppermute | solution.py:18
  40.9 1.0 pad_maximum_fusion.1
  42.0 0.7 all-gather.7.cloned.1.call-update
  42.7 26.3 %all-gather.5.cloned.1.call-done = bf16[4,1,10,32,1280]{4,3,2,1,0:T(8,128)(2,1)} async-done(((bf16[1,1,10,32,1280]{4,3,2,1,0:T(8,128)(2,1)}), bf16[4,1,10,32,1280]{4,3,2,1,0:T(8,128)(2,1)}) %all-gather.5.cloned.1.call-update) | async-done | bytes 3276816 | tf_op jit(solution)/shard_map/all_gather | solution.py:82
  69.0 19.4 %pad_slice_fusion = (bf16[4,1,8,32,1280]{4,3,2,1,0:T(8,128)(2,1)S(1)}, bf16[4,1,8,32,1280]{4,3,2,1,0:T(8,128)(2,1)}, bf16[4,1,8,32,1280]{4,3,2,1,0:T(8,128)(2,1)...) fusion(bf16[4,1,10,32,1280]{4,3,2,1,0:T(8,128)(2,1)} %all-gathe, ...), kind=kLoop, calls=%fused_computation | loop fusion | bytes 34734080 | tf_op jit(solution)/shard_map/slice | solution.py:46
  88.3 115.2 %all-gather.7.cloned.1.call-done = bf16[9,1280,320]{1,2,0:T(8,128)(2,1)} async-done(((bf16[9,1280,80]{1,2,0:T(8,128)(2,1)}), bf16[9,1280,320]{1,2,0:T(8,128)(2,1)}) %all-gather.7.cloned.1.call-update) | async-done | bytes 7372816 | tf_op jit(solution)/shard_map/all_gather | solution.py:85
  203.6 3.1 fusion.18
  206.7 3.0 convolution_add_fusion.9
  209.7 1.0 convolution_add_fusion.8
  210.8 0.7 copy-done.5
  211.5 1.0 convolution_add_fusion.7
  212.5 0.7 copy-done.4
  213.2 1.0 convolution_add_fusion.6
  214.3 0.7 copy-done.3
  215.0 1.0 convolution_add_fusion.5
  216.0 0.7 copy-done.2
  216.7 1.0 convolution_add_fusion.4
  217.8 0.7 copy-done.1
  218.4 1.0 convolution_add_fusion.3
  219.5 1.1 fusion.4
  220.6 1.2 copy.24
  221.7 3.5 all-to-all-start
  225.4 11.5 %all-to-all-done = bf16[4,1,8,32,320]{4,3,2,1,0:T(8,128)(2,1)S(1)} async-done(((bf16[4,1,8,32,320]{4,3,2,1,0:T(8,128)(2,1)}), bf16[4,1,8,32,320]{4,3,2,1,0:T(8,128)(2,1)S(1)}, u32[]{:S(2)}, u32[]{:S(2)}) %all-to-all-start) | async-done | bytes 655392 | tf_op jit(solution)/shard_map/all_to_all | solution.py:87
  237.5 18.8 %all-reduce.1 = (f32[1,32]{1,0:T(1,128)S(1)}, f32[1,32]{1,0:T(1,128)S(1)}) all-reduce(f32[1,32]{1,0:T(1,128)S(1)} %bitcast.113, f32[1,32]{1,0:T(1,128)S(1)} %bitcast.111), channel_id=1, replica_groups=mesh['rep'=4,'frame'=4,'row'=2] {'frame','row'}, use_global_device_ids=true, to_apply=%region_11.12 | all-reduce | flops 64 | bytes 512 | tf_op jit(solution)/shard_map/psum | solution.py:29
  256.8 1.0 copy.26
  257.9 0.9 reshape.227
  259.3 1.3 collective-permute-start.2
  260.6 1.3 collective-permute-start.3
  261.9 8.9 %collective-permute-done.2 = bf16[1,1,8,32,1280]{4,3,2,1,0:T(8,128)(2,1)S(1)} collective-permute-done((bf16[1,1,8,32,1280]{4,3,2,1,0:T(8,128)(2,1)S(1)}, bf16[1,1,8,32,1280]{4,3,2,1,0:T(8,128)(2,1)S(1)}, u32[]{:S(2)}, u32[]{:S(2)}) %collective-permute-start.2) | collective-permute-done | bytes 655392 | tf_op jit(solution)/shard_map/ppermute | solution.py:15
  270.8 4.2 %collective-permute-done.3 = bf16[1,1,8,32,1280]{4,3,2,1,0:T(8,128)(2,1)S(1)} collective-permute-done((bf16[1,1,8,32,1280]{4,3,2,1,0:T(8,128)(2,1)S(1)}, bf16[1,1,8,32,1280]{4,3,2,1,0:T(8,128)(2,1)S(1)}, u32[]{:S(2)}, u32[]{:S(2)}) %collective-permute-start.3) | collective-permute-done | bytes 655392 | tf_op jit(solution)/shard_map/ppermute | solution.py:18
  274.9 1.6 pad_maximum_fusion
  276.6 0.5 all-gather.11.cloned.1.call-update
  277.1 52.2 %all-gather.9.cloned.1.call-done = bf16[4,3,8,32,1280]{4,3,2,1,0:T(8,128)(2,1)} async-done(((bf16[1,3,8,32,1280]{4,3,2,1,0:T(8,128)(2,1)}), bf16[4,3,8,32,1280]{4,3,2,1,0:T(8,128)(2,1)}) %all-gather.9.cloned.1.call-update) | async-done | bytes 7864336 | tf_op jit(solution)/shard_map/all_gather | solution.py:93
  329.3 5.2 %fusion.19 = (bf16[4,1,8,32,1280]{4,3,2,1,0:T(8,128)(2,1)S(1)}, bf16[4,1,8,32,1280]{4,3,2,1,0:T(8,128)(2,1)}, bf16[4,1,8,32,1280]{4,3,2,1,0:T(8,128)(2,1)}) fusion(bf16[4,3,8,32,1280]{4,3,2,1,0:T(8,128)(2,1)} %all-gather.9.cloned.1.call-done), kind=kLoop, calls=%fused_computation.61 | loop fusion | bytes 15728640 | tf_op jit(solution)/shard_map/slice | solution.py:60
  334.5 48.2 %all-gather.11.cloned.1.call-done = bf16[3,1280,320]{1,2,0:T(8,128)(2,1)} async-done(((bf16[3,1280,80]{1,2,0:T(8,128)(2,1)}), bf16[3,1280,320]{1,2,0:T(8,128)(2,1)}) %all-gather.11.cloned.1.call-update) | async-done | bytes 2457616 | tf_op jit(solution)/shard_map/all_gather | solution.py:95
  382.7 3.1 fusion.17
  386.2 1.0 convolution_add_fusion.1
  387.3 1.0 fusion.5
  388.7 14.2 %all_to_all.8 = bf16[4,1,8,32,320]{4,3,2,1,0:T(8,128)(2,1)S(1)} all-to-all(bf16[4,1,8,32,320]{4,3,2,1,0:T(8,128)(2,1)S(1)} %bitcast.98), channel_id=1, replica_groups=mesh['rep'=4,'frame'=4,'row'=2] {'rep'}, dimensions={0} | all-to-all | bytes 1310720 | tf_op jit(solution)/shard_map/all_to_all | solution.py:97
  403.0 1.0 copy.29
  404.1 0.9 reshape.228
  405.1 1.2 fusion.16
  (56 shorter events, 3.8 us)
Async XLA Ops:
  6.5 62.4 %all-gather.5.cloned.1.call-start = ((), (), s32[]{:S(2)}) async-start(), calls=%async_computation.2 | async-start | bytes 4096000 | tf_op jit(solution)/shard_map/all_gather | solution.py:82
  33.3 3.3 collective-permute-start
  34.6 6.3 %collective-permute-start.1 = (bf16[1,1,1,32,1280]{4,3,2,1,0:T(8,128)(2,1)S(1)}, bf16[1,1,1,32,1280]{4,3,2,1,0:T(8,128)(2,1)S(1)}, u32[]{:S(2)}, u32[]{:S(2)}) collective-permute-start(bf16[1,1,1,32,1280]{4,3,2,1,0:T(8,128)(2,1)S(1)} %get-tuple-element.26), channel_id=1, source_target_pairs={{1,0},{3,2},{5,4},{7,6},{9,8},{11,10},{13,12},{15,14},{17,16},{19,... | collective-permute-start | bytes 245768 | tf_op jit(solution)/shard_map/ppermute | solution.py:18
  42.0 161.6 %all-gather.7.cloned.1.call-start = ((), (), s32[]{:S(2)}) async-start(), calls=%async_computation.3 | async-start | bytes 9216000 | tf_op jit(solution)/shard_map/all_gather | solution.py:85
  203.6 3.1 copy-start.7
  203.6 6.1 %copy-start.13 = (bf16[9,1280,320]{1,2,0:T(8,128)(2,1)S(1)}, bf16[9,1280,320]{1,2,0:T(8,128)(2,1)}, u32[]{:S(2)}) copy-start(bf16[9,1280,320]{1,2,0:T(8,128)(2,1)} %all-gather.7.cloned.1.call-done) | copy-start | bytes 22118404
  206.7 3.0 copy-start.6
  209.7 1.7 copy-start.5
  211.5 1.7 copy-start.4
  213.2 1.7 copy-start.3
  215.0 1.7 copy-start.2
  216.7 1.7 copy-start.1
  220.6 4.7 %copy-start.9 = (f32[1280]{0:T(1024)S(1)}, f32[1280]{0:T(1024)}, u32[]{:S(2)}) copy-start(f32[1280]{0:T(1024)} %param.14) | copy-start | bytes 15364
  221.7 15.1 %all-to-all-start = ((bf16[4,1,8,32,320]{4,3,2,1,0:T(8,128)(2,1)}), bf16[4,1,8,32,320]{4,3,2,1,0:T(8,128)(2,1)S(1)}, u32[]{:S(2)}, u32[]{:S(2)}) async-start(bf16[4,1,8,32,320]{4,3,2,1,0:T(8,128)(2,1)} %bitcast.23), calls=%async_computation | async-start | bytes 1572864 | tf_op jit(solution)/shard_map/all_to_all | solution.py:87
  225.2 104.1 %all-gather.9.cloned.1.call-start = ((), (), s32[]{:S(2)}) async-start(), calls=%async_computation.4 | async-start | bytes 9830400 | tf_op jit(solution)/shard_map/all_gather | solution.py:93
  257.9 0.9 copy-start.10
  257.9 0.9 copy-start.11
  259.3 11.5 %collective-permute-start.2 = (bf16[1,1,8,32,1280]{4,3,2,1,0:T(8,128)(2,1)S(1)}, bf16[1,1,8,32,1280]{4,3,2,1,0:T(8,128)(2,1)S(1)}, u32[]{:S(2)}, u32[]{:S(2)}) collective-permute-start(bf16[1,1,8,32,1280]{4,3,2,1,0:T(8,128)(2,1)S(1)} %multiply_convert_fusion), channel_id=1, source_target_pairs={{0,2},{2,4},{4,6},{1,3},{3,5},{5,7},{8,10},{10,12},{12,14},{9,11},... | collective-permute-start | bytes 1966088 | tf_op jit(solution)/shard_map/ppermute | solution.py:15
  260.6 14.3 %collective-permute-start.3 = (bf16[1,1,8,32,1280]{4,3,2,1,0:T(8,128)(2,1)S(1)}, bf16[1,1,8,32,1280]{4,3,2,1,0:T(8,128)(2,1)S(1)}, u32[]{:S(2)}, u32[]{:S(2)}) collective-permute-start(bf16[1,1,8,32,1280]{4,3,2,1,0:T(8,128)(2,1)S(1)} %multiply_convert_fusion), channel_id=1, source_target_pairs={{2,0},{4,2},{6,4},{3,1},{5,3},{7,5},{10,8},{12,10},{14,12},{11,9},... | collective-permute-start | bytes 1966088 | tf_op jit(solution)/shard_map/ppermute | solution.py:18
  276.5 106.2 %all-gather.11.cloned.1.call-start = ((), (), s32[]{:S(2)}) async-start(), calls=%async_computation.5 | async-start | bytes 3072000 | tf_op jit(solution)/shard_map/all_gather | solution.py:95
  382.7 3.1 copy-start.8
  382.7 3.5 copy-start.14
  404.1 1.1 copy-start
  404.1 1.1 copy-start.12
Sparse Core Ops, SparseCore 0:
  42.1 26.8 all-gather.4
  70.5 132.9 all-gather.6
  276.7 52.6 all-gather.8
  330.8 51.8 all-gather.10
where the time goes:
time: 413 us
  waiting for transfers between devices  273 us (66%)
  blocking collectives  56.1 us (14%)
  local copies, waits for them, and re-layouts  35 us (8%)
  matrix products  18.6 us (5%)
  between operations  13.5 us (3%)
  starting transfers between devices  8.83 us (2%)
  other arithmetic  8.25 us (2%)
    all_gather x1, waiting for transfers between devices, shards(): lax.all_gather(spatial_weight, 'frame', axis=2, tiled=True)  115 us
    all_gather x1, waiting for transfers between devices, shards(): window_all = lax.all_gather(window, 'rep', axis=0, tiled=True)  52.2 us
    all_gather x1, waiting for transfers between devices, shards(): lax.all_gather(temporal_weight, 'frame', axis=2, tiled=True)  48.2 us
    psum x2, blocking collectives, norm_silu(): sums, squares = lax.psum((sums, squares), ('frame', 'row'))  41.9 us
    all_gather x1, waiting for transfers between devices, shards(): gathered = lax.all_gather(with_rims, 'rep', axis=0, tiled=True)  26.3 us
    slice x1, local copies, waits for them, and re-layouts, conv_taps(): padded[:, :, row_tap:row_tap + rows, col_tap:col_tap + cols, :]  19.4 us
    all_to_all x1, blocking collectives, shards(): lax.all_to_all(quarter_time.astype(jnp.bfloat16), 'rep', split_axis=0, co...  14.2 us
    dot_general x9, matrix products, conv_taps(): jnp.dot(section, weights[3 * row_tap + col_tap], preferred_element_type=j...  13.4 us
  transfers between devices with their start and end apart: 9, of which 9 were waited for; matrix products, arithmetic and copies ran while one was open for 6% of the time, Pallas kernels for 0%

commit v1 on v0

--- a/solution.py
+++ b/solution.py
@@ -5,6 +5,32 @@
 
 GROUPS = 32
 EPS = 1e-05
+
+
+def _fix_quotas(packet, ndim_at):
+    current_block = list(packet.shape[1:])
+    current_block[ndim_at] *= packet.shape[0]
+    return jnp.moveaxis(packet, 0, ndim_at).reshape(current_block)
+
+
+def fix_the_sums_all(chip_axis, k_dim, arr_in):
+    extent = lax.psum(1, chip_axis)
+    a_now = range(extent)
+    state_next = map(lambda k: (k, (k + 1) % extent), a_now)
+    line_up = list(state_next)
+    ledger = [(ii, to_i) for to_i, ii in line_up]
+    earlier, local_out = ([], [])
+    for w in tuple(range(extent - 1)):
+        if w % 2 == 0:
+            earlier.append(lax.ppermute(earlier[-1] if earlier else arr_in, chip_axis, line_up))
+        else:
+            clean = lax.ppermute(local_out[-1] if local_out else arr_in, chip_axis, ledger)
+            local_out.append(clean)
+    w1 = jnp.stack([*earlier[::-1], arr_in, *local_out], axis=0)
+    t_next = lax.axis_index(chip_axis)
+    n_now = t_next - len(earlier)
+    w1 = w1[(jnp.arange(extent) - n_now) % extent]
+    return _fix_quotas(w1, k_dim)
 
 
 def padded_2(block, sides, width):
@@ -79,7 +105,7 @@
     inputs = activations.astype(jnp.float32)
     first = norm_silu(inputs, first_gain, first_shift)
     with_rims = padded_2(first, (("row", 2),), 1)
-    gathered = lax.all_gather(with_rims, "rep", axis=0, tiled=True)
+    gathered = fix_the_sums_all("rep", 0, with_rims)
     padded = jnp.pad(gathered, ((0, 0), (0, 0), (0, 0), (1, 1), (0, 0)))
     quarter = conv_taps(
         padded, lax.all_gather(spatial_weight, "frame", axis=2, tiled=True), rows_dev, cols

time: 413 us -> 355 us (0.86)
  waiting for transfers between devices: 273 us -> 219 us
  local copies, waits for them, and re-layouts: 35 us -> 27.4 us
    all_gather x1, waiting for transfers between devices: 115 us -> 58.6 us  [shards(): lax.all_gather(spatial_weight, 'frame', axis=2, tiled=True)]
    ppermute x0 -> x3, waiting for transfers between devices: none -> 28.8 us  [the longest x2 28.1 us: fix_the_sums_all(): lax.ppermute(earlier[-1] if earlier else arr_in, chip_axis, line_up)]
    all_gather x1 -> x0, waiting for transfers between devices: 26.3 us -> none  [shards(): gathered = lax.all_gather(with_rims, 'rep', axis=0, tiled=True)]
    slice x1, local copies, waits for them, and re-layouts: 19.4 us -> 8.52 us  [conv_taps(): padded[:, :, row_tap:row_tap + rows, col_tap:col_tap + cols, :]]
  transfers between devices with their start and end apart: 9 -> 11, of which waited for: 9 -> 11; matrix products, arithmetic and copies ran while one was open for 6% -> 6% of each run, Pallas kernels for 0% -> 0%
where the time goes in v1:
time: 355 us
  waiting for transfers between devices  219 us (62%)
  blocking collectives  56.8 us (16%)
  local copies, waits for them, and re-layouts  27.4 us (8%)
  matrix products  18.6 us (5%)
  between operations  13.5 us (4%)
  starting transfers between devices  10.7 us (3%)
  other arithmetic  9.14 us (3%)
    all_gather x1, waiting for transfers between devices, shards(): lax.all_gather(spatial_weight, 'frame', axis=2, tiled=True)  58.6 us
    all_gather x1, waiting for transfers between devices, shards(): window_all = lax.all_gather(window, 'rep', axis=0, tiled=True)  51.6 us
    all_gather x1, waiting for transfers between devices, shards(): lax.all_gather(temporal_weight, 'frame', axis=2, tiled=True)  48.3 us
    psum x2, blocking collectives, norm_silu(): sums, squares = lax.psum((sums, squares), ('frame', 'row'))  42.6 us
    ppermute x2, waiting for transfers between devices, fix_the_sums_all(): lax.ppermute(earlier[-1] if earlier else arr_in, chip_axis, line_up)  28.1 us
    all_to_all x1, blocking collectives, shards(): lax.all_to_all(quarter_time.astype(jnp.bfloat16), 'rep', split_axis=0, co...  14.2 us
    dot_general x9, matrix products, conv_taps(): jnp.dot(section, weights[3 * row_tap + col_tap], preferred_element_type=j...  13.4 us
    all_to_all x1, waiting for transfers between devices, shards(): lax.all_to_all(quarter.astype(jnp.bfloat16), 'rep', split_axis=0, concat_...  11.5 us
  transfers between devices with their start and end apart: 11, of which 11 were waited for; matrix products, arithmetic and copies ran while one was open for 6% of the time, Pallas kernels for 0%

profile of v1, /device:TPU:0, one launch (start us, length us, event | category | flops | bytes accessed | tf_op | source)
XLA Modules:
  0.0 354.6 jit_solution(11678706592531798918)
XLA Ops:
  6.5 0.7 all-gather.4.cloned.1.call-update
  7.3 1.3 convert_reduce_fusion
  8.9 23.7 %all-reduce.2 = (f32[1,32]{1,0:T(1,128)S(1)}, f32[1,32]{1,0:T(1,128)S(1)}) all-reduce(f32[1,32]{1,0:T(1,128)S(1)} %bitcast.128, f32[1,32]{1,0:T(1,128)S(1)} %bitcast.126), channel_id=1, replica_groups=mesh['rep'=4,'frame'=4,'row'=2] {'frame','row'}, use_global_device_ids=true, to_apply=%region_5.6 | all-reduce | flops 64 | bytes 512 | tf_op jit(solution)/shard_map/psum | solution.py:55
  33.5 1.3 collective-permute-start
  34.8 1.3 collective-permute-start.1
  36.1 0.7 collective-permute-done
  36.9 4.3 %collective-permute-done.1 = bf16[1,1,1,32,1280]{4,3,2,1,0:T(8,128)(2,1)S(1)} collective-permute-done((bf16[1,1,1,32,1280]{4,3,2,1,0:T(8,128)(2,1)S(1)}, bf16[1,1,1,32,1280]{4,3,2,1,0:T(8,128)(2,1)S(1)}, u32[]{:S(2)}, u32[]{:S(2)}) %collective-permute-start.1) | collective-permute-done | bytes 81952 | tf_op jit(solution)/shard_map/ppermute | solution.py:44
  41.2 1.0 fusion.21
  42.2 1.7 collective-permute-start.4
  43.9 17.2 %collective-permute-done.2 = bf16[1,1,10,32,1280]{4,3,2,1,0:T(8,128)(2,1)S(1)} collective-permute-done((bf16[1,1,10,32,1280]{4,3,2,1,0:T(8,128)(2,1)}, bf16[1,1,10,32,1280]{4,3,2,1,0:T(8,128)(2,1)S(1)}, u32[]{:S(2)}, u32[]{:S(2)}) %collective-permute-start.2) | collective-permute-done | bytes 819232 | tf_op jit(solution)/shard_map/ppermute | solution.py:25
  62.1 10.9 %collective-permute-done.3 = bf16[1,1,10,32,1280]{4,3,2,1,0:T(8,128)(2,1)S(1)} collective-permute-done((bf16[1,1,10,32,1280]{4,3,2,1,0:T(8,128)(2,1)S(1)}, bf16[1,1,10,32,1280]{4,3,2,1,0:T(8,128)(2,1)S(1)}, u32[]{:S(2)}, u32[]{:S(2)}) %collective-permute-start.3) | collective-permute-done | bytes 819232 | tf_op jit(solution)/shard_map/ppermute | solution.py:25
  72.9 2.0 maximum_bitcast_fusion
  74.9 2.7 gather_fusion
  77.6 8.5 %pad_slice_fusion = (bf16[4,1,8,32,1280]{4,3,2,0,1:T(8,128)(2,1)}, bf16[4,1,8,32,1280]{4,3,2,0,1:T(8,128)(2,1)}, bf16[4,1,8,32,1280]{4,3,2,0,1:T(8,128)(2,1)}, b...) fusion(bf16[4,1,10,32,1280]{4,3,2,0,1:T(8,128)(2,1)S(1)} %bitca, ...), kind=kLoop, calls=%fused_computation.1 | loop fusion | bytes 34734080 | tf_op jit(solution)/shard_map/slice | solution.py:72
  86.1 58.6 %all-gather.4.cloned.1.call-done = bf16[9,1280,320]{1,2,0:T(8,128)(2,1)} async-done(((bf16[9,1280,80]{1,2,0:T(8,128)(2,1)}), bf16[9,1280,320]{1,2,0:T(8,128)(2,1)}) %all-gather.4.cloned.1.call-update) | async-done | bytes 7372816 | tf_op jit(solution)/shard_map/all_gather | solution.py:111
  144.7 3.1 fusion.18
  147.8 3.0 convolution_add_fusion.9
  150.8 1.0 convolution_add_fusion.8
  152.6 1.0 convolution_add_fusion.7
  153.6 0.7 copy-done.6
  154.3 1.0 convolution_add_fusion.6
  156.0 1.0 convolution_add_fusion.5
  157.1 0.7 copy-done.4
  157.8 1.0 convolution_add_fusion.4
  158.8 0.7 copy-done.3
  159.5 1.0 convolution_add_fusion.3
  161.3 1.0 fusion.4
  162.3 1.2 copy.24
  163.5 3.5 all-to-all-start
  167.1 11.5 %all-to-all-done = bf16[4,1,8,32,320]{4,3,2,1,0:T(8,128)(2,1)S(1)} async-done(((bf16[4,1,8,32,320]{4,3,2,1,0:T(8,128)(2,1)}), bf16[4,1,8,32,320]{4,3,2,1,0:T(8,128)(2,1)S(1)}, u32[]{:S(2)}, u32[]{:S(2)}) %all-to-all-start) | async-done | bytes 655392 | tf_op jit(solution)/shard_map/all_to_all | solution.py:113
  179.3 18.9 %all-reduce.1 = (f32[1,32]{1,0:T(1,128)S(1)}, f32[1,32]{1,0:T(1,128)S(1)}) all-reduce(f32[1,32]{1,0:T(1,128)S(1)} %bitcast.127, f32[1,32]{1,0:T(1,128)S(1)} %bitcast.125), channel_id=1, replica_groups=mesh['rep'=4,'frame'=4,'row'=2] {'frame','row'}, use_global_device_ids=true, to_apply=%region_11.12 | all-reduce | flops 64 | bytes 512 | tf_op jit(solution)/shard_map/psum | solution.py:55
  198.7 1.0 copy.26
  199.7 0.9 reshape.280
  201.1 1.3 collective-permute-start.5
  202.5 1.3 collective-permute-start.6
  203.8 9.2 %collective-permute-done.5 = bf16[1,1,8,32,1280]{4,3,2,1,0:T(8,128)(2,1)S(1)} collective-permute-done((bf16[1,1,8,32,1280]{4,3,2,1,0:T(8,128)(2,1)S(1)}, bf16[1,1,8,32,1280]{4,3,2,1,0:T(8,128)(2,1)S(1)}, u32[]{:S(2)}, u32[]{:S(2)}) %collective-permute-start.5) | collective-permute-done | bytes 655392 | tf_op jit(solution)/shard_map/ppermute | solution.py:41
  213.0 4.2 %collective-permute-done.6 = bf16[1,1,8,32,1280]{4,3,2,1,0:T(8,128)(2,1)S(1)} collective-permute-done((bf16[1,1,8,32,1280]{4,3,2,1,0:T(8,128)(2,1)S(1)}, bf16[1,1,8,32,1280]{4,3,2,1,0:T(8,128)(2,1)S(1)}, u32[]{:S(2)}, u32[]{:S(2)}) %collective-permute-start.6) | collective-permute-done | bytes 655392 | tf_op jit(solution)/shard_map/ppermute | solution.py:44
  217.1 1.6 pad_maximum_fusion
  219.4 51.6 %all-gather.6.cloned.1.call-done = bf16[4,3,8,32,1280]{4,3,2,1,0:T(8,128)(2,1)} async-done(((bf16[1,3,8,32,1280]{4,3,2,1,0:T(8,128)(2,1)}), bf16[4,3,8,32,1280]{4,3,2,1,0:T(8,128)(2,1)}) %all-gather.6.cloned.1.call-update) | async-done | bytes 7864336 | tf_op jit(solution)/shard_map/all_gather | solution.py:119
  271.1 5.2 %fusion.22 = (bf16[4,1,8,32,1280]{4,3,2,1,0:T(8,128)(2,1)S(1)}, bf16[4,1,8,32,1280]{4,3,2,1,0:T(8,128)(2,1)}, bf16[4,1,8,32,1280]{4,3,2,1,0:T(8,128)(2,1)}) fusion(bf16[4,3,8,32,1280]{4,3,2,1,0:T(8,128)(2,1)} %all-gather.6.cloned.1.call-done), kind=kLoop, calls=%fused_computation.71 | loop fusion | bytes 15728640 | tf_op jit(solution)/shard_map/slice | solution.py:86
  276.3 48.3 %all-gather.8.cloned.1.call-done = bf16[3,1280,320]{1,2,0:T(8,128)(2,1)} async-done(((bf16[3,1280,80]{1,2,0:T(8,128)(2,1)}), bf16[3,1280,320]{1,2,0:T(8,128)(2,1)}) %all-gather.8.cloned.1.call-update) | async-done | bytes 2457616 | tf_op jit(solution)/shard_map/all_gather | solution.py:121
  324.6 3.1 fusion.17
  328.1 1.0 convolution_add_fusion.1
  329.1 1.1 fusion.5
  330.6 14.2 %all_to_all.8 = bf16[4,1,8,32,320]{4,3,2,1,0:T(8,128)(2,1)S(1)} all-to-all(bf16[4,1,8,32,320]{4,3,2,1,0:T(8,128)(2,1)S(1)} %bitcast.109), channel_id=1, replica_groups=mesh['rep'=4,'frame'=4,'row'=2] {'rep'}, dimensions={0} | all-to-all | bytes 1310720 | tf_op jit(solution)/shard_map/all_to_all | solution.py:123
  344.9 1.0 copy.29
  346.0 0.9 reshape.281
  346.9 1.2 fusion.16
  (71 shorter events, 7.7 us)
Async XLA Ops:
  6.5 26.5 %copy-start = (bf16[1,1,8,32,1280]{4,3,2,1,0:T(8,128)(2,1)S(1)}, bf16[1,1,8,32,1280]{4,3,2,1,0:T(8,128)(2,1)}, u32[]{:S(2)}) copy-start(bf16[1,1,8,32,1280]{4,3,2,1,0:T(8,128)(2,1)} %param.9) | copy-start | bytes 1966084
  6.5 26.5 %copy-start.13 = (f32[1280]{0:T(1024)S(1)}, f32[1280]{0:T(1024)}, u32[]{:S(2)}) copy-start(f32[1280]{0:T(1024)} %param.12) | copy-start | bytes 15364
  6.5 26.5 %copy-start.12 = (f32[1280]{0:T(1024)S(1)}, f32[1280]{0:T(1024)}, u32[]{:S(2)}) copy-start(f32[1280]{0:T(1024)} %param.13) | copy-start | bytes 15364
  6.5 138.1 %all-gather.4.cloned.1.call-start = ((), (), s32[]{:S(2)}) async-start(), calls=%async_computation.2 | async-start | bytes 9216000 | tf_op jit(solution)/shard_map/all_gather | solution.py:111
  33.5 3.3 collective-permute-start
  34.8 6.3 %collective-permute-start.1 = (bf16[1,1,1,32,1280]{4,3,2,1,0:T(8,128)(2,1)S(1)}, bf16[1,1,1,32,1280]{4,3,2,1,0:T(8,128)(2,1)S(1)}, u32[]{:S(2)}, u32[]{:S(2)}) collective-permute-start(bf16[1,1,1,32,1280]{4,3,2,1,0:T(8,128)(2,1)S(1)} %get-tuple-element.28), channel_id=1, source_target_pairs={{1,0},{3,2},{5,4},{7,6},{9,8},{11,10},{13,12},{15,14},{17,16},{19,... | collective-permute-start | bytes 245768 | tf_op jit(solution)/shard_map/ppermute | solution.py:44
  42.2 19.0 %collective-permute-start.2 = (bf16[1,1,10,32,1280]{4,3,2,1,0:T(8,128)(2,1)}, bf16[1,1,10,32,1280]{4,3,2,1,0:T(8,128)(2,1)S(1)}, u32[]{:S(2)}, u32[]{:S(2)}) collective-permute-start(bf16[1,1,10,32,1280]{4,3,2,1,0:T(8,128)(2,1)} %get-tuple-element.26), channel_id=1, source_target_pairs={{0,8},{8,16},{16,24},{24,0},{1,9},{9,17},{17,25},{25,1},{2,10},{10... | collective-permute-start | bytes 2457608 | tf_op jit(solution)/shard_map/ppermute | solution.py:25
  42.2 19.9 %collective-permute-start.4 = (bf16[1,1,10,32,1280]{4,3,2,1,0:T(8,128)(2,1)}, bf16[1,1,10,32,1280]{4,3,2,1,0:T(8,128)(2,1)S(1)}, u32[]{:S(2)}, u32[]{:S(2)}) collective-permute-start(bf16[1,1,10,32,1280]{4,3,2,1,0:T(8,128)(2,1)} %get-tuple-element.26), channel_id=1, source_target_pairs={{8,0},{16,8},{24,16},{0,24},{9,1},{17,9},{25,17},{1,25},{10,2},{18... | collective-permute-start | bytes 2457608 | tf_op jit(solution)/shard_map/ppermute | solution.py:27
  61.1 11.8 %collective-permute-start.3 = (bf16[1,1,10,32,1280]{4,3,2,1,0:T(8,128)(2,1)S(1)}, bf16[1,1,10,32,1280]{4,3,2,1,0:T(8,128)(2,1)S(1)}, u32[]{:S(2)}, u32[]{:S(2)}) collective-permute-start(bf16[1,1,10,32,1280]{4,3,2,1,0:T(8,128)(2,1)S(1)} %collective-permute-done.2), channel_id=1, source_target_pairs={{0,8},{8,16},{16,24},{24,0},{1,9},{9,17},{17,25},{25,1},{2,10},{10... | collective-permute-start | bytes 2457608 | tf_op jit(solution)/shard_map/ppermute | solution.py:25
  144.7 3.1 copy-start.9
  144.7 6.1 %copy-start.17 = (bf16[9,1280,320]{1,2,0:T(8,128)(2,1)S(1)}, bf16[9,1280,320]{1,2,0:T(8,128)(2,1)}, u32[]{:S(2)}) copy-start(bf16[9,1280,320]{1,2,0:T(8,128)(2,1)} %all-gather.4.cloned.1.call-done) | copy-start | bytes 22118404
  147.8 3.0 copy-start.8
  150.8 1.7 copy-start.7
  152.6 1.7 copy-start.6
  154.3 1.7 copy-start.5
  156.0 1.7 copy-start.4
  157.8 1.7 copy-start.3
  159.5 1.7 copy-start.2
  162.3 4.7 %copy-start.11 = (f32[1280]{0:T(1024)S(1)}, f32[1280]{0:T(1024)}, u32[]{:S(2)}) copy-start(f32[1280]{0:T(1024)} %param.14) | copy-start | bytes 15364
  163.5 15.1 %all-to-all-start = ((bf16[4,1,8,32,320]{4,3,2,1,0:T(8,128)(2,1)}), bf16[4,1,8,32,320]{4,3,2,1,0:T(8,128)(2,1)S(1)}, u32[]{:S(2)}, u32[]{:S(2)}) async-start(bf16[4,1,8,32,320]{4,3,2,1,0:T(8,128)(2,1)} %bitcast.30), calls=%async_computation | async-start | bytes 1572864 | tf_op jit(solution)/shard_map/all_to_all | solution.py:113
  167.0 104.1 %all-gather.6.cloned.1.call-start = ((), (), s32[]{:S(2)}) async-start(), calls=%async_computation.3 | async-start | bytes 9830400 | tf_op jit(solution)/shard_map/all_gather | solution.py:119
  198.7 2.0 copy-start.14
  198.7 2.0 copy-start.15
  201.1 11.8 %collective-permute-start.5 = (bf16[1,1,8,32,1280]{4,3,2,1,0:T(8,128)(2,1)S(1)}, bf16[1,1,8,32,1280]{4,3,2,1,0:T(8,128)(2,1)S(1)}, u32[]{:S(2)}, u32[]{:S(2)}) collective-permute-start(bf16[1,1,8,32,1280]{4,3,2,1,0:T(8,128)(2,1)S(1)} %multiply_convert_fusion), channel_id=1, source_target_pairs={{0,2},{2,4},{4,6},{1,3},{3,5},{5,7},{8,10},{10,12},{12,14},{9,11},... | collective-permute-start | bytes 1966088 | tf_op jit(solution)/shard_map/ppermute | solution.py:41
  202.5 14.6 %collective-permute-start.6 = (bf16[1,1,8,32,1280]{4,3,2,1,0:T(8,128)(2,1)S(1)}, bf16[1,1,8,32,1280]{4,3,2,1,0:T(8,128)(2,1)S(1)}, u32[]{:S(2)}, u32[]{:S(2)}) collective-permute-start(bf16[1,1,8,32,1280]{4,3,2,1,0:T(8,128)(2,1)S(1)} %multiply_convert_fusion), channel_id=1, source_target_pairs={{2,0},{4,2},{6,4},{3,1},{5,3},{7,5},{10,8},{12,10},{14,12},{11,9},... | collective-permute-start | bytes 1966088 | tf_op jit(solution)/shard_map/ppermute | solution.py:44
  218.7 105.9 %all-gather.8.cloned.1.call-start = ((), (), s32[]{:S(2)}) async-start(), calls=%async_computation.4 | async-start | bytes 3072000 | tf_op jit(solution)/shard_map/all_gather | solution.py:121
  324.6 3.1 copy-start.10
  324.6 3.5 copy-start.18
  344.9 2.0 copy-start.1
  344.9 2.0 copy-start.16
Sparse Core Ops, SparseCore 0:
  8.9 135.7 all-gather.3
  218.8 52.2 all-gather.5
  272.6 51.8 all-gather.7
